TPU v7x, 256 devices: a whole 4x4x8 slice. The times are simulated.
256 devices in a mesh: section: 2 (over core), patch: 4 (over y), req: 32 (over z, x).
Axes of the slice: x: 4, y: 4, z: 8, core: 2. Of those that a mesh axis runs over, the one named last changes fastest.
Arguments:
- hidden: bfloat16 [64, 1024, 1536], P('req', 'patch'), may hold values from -6 to 6
- w_qkv: bfloat16 [2, 1536, 2304], P('section', ('patch', 'req')), may hold values from -0.15625 to 0.15625
- w_out: bfloat16 [2, 768, 1536], P('section', ('patch', 'req')), may hold values from -0.21875 to 0.21875
- modulation: float32 [2, 64, 3, 1536], P('section', 'req'), may hold values from -3 to 3
- text_kv: bfloat16 [2, 64, 160, 1536], P('section', 'req'), may hold values from -1000 to 1000
- text_lengths: int32 [64], P('req'), may hold values from 77 to 154, as said below
- stale_kv: bfloat16 [2, 64, 1024, 1536], P('section', 'req', 'patch'), may hold values from -48 to 48
- held_hidden: bfloat16 [2, 64, 96, 1536], P('section', 'req', 'patch'), may hold values from -6 to 6
- recompute_rows: int32 [2, 64, 96], P('section', 'req', 'patch'), may hold values from 0 to 255, as said below
- coefficients: float32 [64, 2], P('req'), may hold values from 0.5 to 1.5
Outputs:
- latents: float32 [64, 1024, 1536], P('req', 'patch', 'section')
- cache: bfloat16 [2, 64, 1024, 1536], P('section', 'req', 'patch')
Inputs may be any that keep to these rules, and one draw needn't show every extreme that they name: `text_lengths`: some request has exactly 154 text tokens and some exactly 77. `recompute_rows`: the row numbers listed for one layer, request and patch are distinct.
All inputs are finite; a program needn't handle non-finite values.
Results may differ from a plain program's by a relative error of at most 0.025.
Values may be sent and summed in bfloat16 or wider, within the bound.
No kernel may reach another device: no remote copies, remote signals or barrier semaphores. Data moves between devices by JAX's collectives and lax.ppermute only.
A program may use at most 128 MiB of HBM per device.

v0:
```python
import jax
import jax.numpy as jnp
from jax import lax
from jax.sharding import PartitionSpec as P

HEADS = 12
norm_eps = 1e-06
score_scale = 0.125


def shifted(block, axis, distance):
    devices = range(lax.axis_size(axis))
    route = [(i - distance, i) for i in devices if i - distance in devices]
    return lax.ppermute(block, axis, route)


def modulate(row_block, shift_row, scale_row):
    values = row_block.astype(jnp.float32)
    centre = values - jnp.mean(values, axis=-1, keepdims=True)
    spread = jnp.mean(centre * centre, axis=-1, keepdims=True)
    return (centre * lax.rsqrt(spread + norm_eps) * (1.0 + scale_row) + shift_row).astype(
        jnp.bfloat16
    )


def attend(queries, key_rows, value_rows, usable):
    row_count = queries.shape[0]
    feature_count = queries.shape[1]
    query_heads = queries.reshape(row_count, HEADS, feature_count // HEADS)
    key_heads = key_rows.reshape(key_rows.shape[0], HEADS, feature_count // HEADS)
    value_heads = value_rows.reshape(value_rows.shape[0], HEADS, feature_count // HEADS)
    scores = (
        jnp.einsum("qhd,khd->hqk", query_heads, key_heads, preferred_element_type=jnp.float32)
        * score_scale
    )
    scores = jnp.where(usable[None, None, :], scores, -1e30)
    row_max = jnp.max(scores, axis=-1, keepdims=True)
    exp_scores = jnp.exp(scores - row_max)
    soft_weights = (exp_scores / jnp.sum(exp_scores, axis=-1, keepdims=True)).astype(jnp.bfloat16)
    attended = jnp.einsum(
        "hqk,khd->qhd", soft_weights, value_heads, preferred_element_type=jnp.float32
    )
    return attended.reshape(row_count, feature_count).astype(jnp.bfloat16)


def body(
    hidden,
    w_qkv,
    w_out,
    modulation,
    text_kv,
    text_lengths,
    stale_kv,
    held_hidden,
    recompute_rows,
    coefficients,
):
    full_qkv, full_out = (
        lax.all_gather(w_qkv[0], ("patch", "req"), axis=0, tiled=True),
        lax.all_gather(w_out[0], ("patch", "req"), axis=0, tiled=True),
    )
    section_index = lax.axis_index("section")
    patch_index = lax.axis_index("patch")
    request_count = hidden.shape[0]
    patch_rows = hidden.shape[1]
    model_width = hidden.shape[2]
    head_width = full_out.shape[0]
    text_slots = text_kv.shape[2]

    def process(layer_input, slot_index):
        mod_rows = lax.dynamic_index_in_dim(modulation[0], slot_index, 0, keepdims=False)
        text_rows = lax.dynamic_index_in_dim(text_kv[0], slot_index, 0, keepdims=False)
        text_count = lax.dynamic_index_in_dim(text_lengths, slot_index, 0, keepdims=False)
        stale_block = lax.dynamic_index_in_dim(stale_kv[0], slot_index, 0, keepdims=False)
        held_rows = lax.dynamic_index_in_dim(held_hidden[0], slot_index, 0, keepdims=False)
        redo_index = lax.dynamic_index_in_dim(recompute_rows[0], slot_index, 0, keepdims=False)
        held_norm = modulate(held_rows, mod_rows[0], mod_rows[1])
        redone = jnp.dot(
            held_norm, full_qkv[:, head_width:], preferred_element_type=jnp.float32
        ).astype(jnp.bfloat16)
        patched = stale_block.at[redo_index].set(redone)
        image_rows = lax.all_gather(patched, "patch", axis=0, tiled=True)
        normed = modulate(layer_input, mod_rows[0], mod_rows[1])
        projected = jnp.dot(normed, full_qkv, preferred_element_type=jnp.float32).astype(
            jnp.bfloat16
        )
        fresh_rows = projected[:, head_width:]
        image_rows = lax.dynamic_update_slice_in_dim(
            image_rows, fresh_rows, patch_index * patch_rows, 0
        )
        context = jnp.concatenate([text_rows, image_rows], axis=0)
        usable = jnp.concatenate(
            [jnp.arange(text_slots) < text_count, jnp.ones((image_rows.shape[0],), jnp.bool_)]
        )
        attended = attend(
            projected[:, :head_width], context[:, :head_width], context[:, head_width:], usable
        )
        update = jnp.dot(attended, full_out, preferred_element_type=jnp.float32)
        layer_out = (layer_input.astype(jnp.float32) + mod_rows[2] * update).astype(jnp.bfloat16)
        return (layer_out, fresh_rows)

    first_pass = [process(hidden[slot_number], slot_number) for slot_number in range(request_count)]
    first_out = jnp.stack([entry[0] for entry in first_pass])
    first_fresh = jnp.stack([entry[1] for entry in first_pass])
    received = shifted(first_out, "section", 1)
    second_pass = [
        process(received[slot_number], slot_number) for slot_number in range(request_count)
    ]
    second_out = jnp.stack([entry[0] for entry in second_pass])
    second_fresh = jnp.stack([entry[1] for entry in second_pass])
    fresh_all = jnp.where(section_index == 0, first_fresh, second_fresh)
    half_width = model_width // 2
    returned = shifted(second_out[:, :, :half_width], "section", -1)
    own_half = jnp.where(section_index == 0, returned, second_out[:, :, half_width:])
    source_half = lax.dynamic_slice_in_dim(hidden, section_index * half_width, half_width, 2)
    latents = coefficients[:, 0][:, None, None] * source_half.astype(jnp.float32) + coefficients[
        :, 1
    ][:, None, None] * own_half.astype(jnp.float32)
    return (latents, fresh_all[None])


def solution(mesh):
    return jax.shard_map(
        body,
        mesh=mesh,
        in_specs=(
            P("req", "patch", None),
            P("section", ("patch", "req"), None),
            P("section", ("patch", "req"), None),
            P("section", "req", None, None),
            P("section", "req", None, None),
            P("req"),
            P("section", "req", "patch", None),
            P("section", "req", "patch", None),
            P("section", "req", "patch"),
            P("req", None),
        ),
        out_specs=(P("req", "patch", "section"), P("section", "req", "patch", None)),
        check_vma=False,
    )
```

profile of v0, /device:TPU:1, one launch (start us, length us, event | category | flops | bytes accessed | tf_op | source)
XLA Modules:
  0.0 496.8 jit_solution(3415797970322674418)
XLA Ops:
  15.7 140.7 %all-gather.11.cloned.1.call-done = bf16[1,1536,2304]{2,0,1:T(2,128)(2,1)} async-done(((bf16[1,12,2304]{2,0,1:T(2,128)(2,1)}), bf16[1,1536,2304]{2,0,1:T(2,128)(2,1)}) %all-gather.11.cloned.1.call-update) | async-done | bytes 7077904 | tf_op jit(solution)/shard_map/all_gather | solution.py:59
  156.4 9.0 %copy.67 = bf16[1,1536,2304]{2,1,0:T(8,128)(2,1)} copy(bf16[1,1536,2304]{2,0,1:T(2,128)(2,1)} %all-gather.11.cloned.1.call-done) | data formatting | bytes 14155776
  165.4 3.1 fusion.52
  170.7 3.2 fusion.55
  180.5 91.4 %all-gather.13.cloned.1.call-done = bf16[1,768,1536]{2,0,1:T(2,128)(2,1)} async-done(((bf16[1,6,1536]{2,0,1:T(2,128)(2,1)}), bf16[1,768,1536]{2,0,1:T(2,128)(2,1)}) %all-gather.13.cloned.1.call-update) | async-done | bytes 2359312 | tf_op jit(solution)/shard_map/all_gather | solution.py:60
  271.9 3.0 copy.65
  275.0 5.2 %convolution_convert_fusion.3 = bf16[256,2304]{1,0:T(8,128)(2,1)S(1)} fusion(bf16[1536,2304]{1,0:T(8,128)(2,1)} %bitcast.210, f32[1536]{0:T(1024)S(1)} %get-tuple-element.16, f32[1536]{0:T(1024)S(1)} %get-tuple-element.17, f32[256]{0:T(256)S(1)} %add_rsqrt_fusion.3, f32[256]{0:T(256)S(1)} %broadcast_multiply_fusion.3, bf16[2,256,1536]{2,1,0:T(8,128)(2,1)S(1)} %copy-done.1), kind=kOutput, calls=%fused_computation.46 | convolution fusion | flops 1814888448 | bytes 9062400 | tf_op jit(solution)/shard_map/dot_general | solution.py:84
  283.9 5.7 %convolution_convert_fusion.2 = bf16[256,2304]{1,0:T(8,128)(2,1)S(1)} fusion(bf16[1536,2304]{1,0:T(8,128)(2,1)} %bitcast.211, f32[1536]{0:T(1024)S(1)} %get-tuple-element.18, f32[1536]{0:T(1024)S(1)} %get-tuple-element.19, f32[256]{0:T(256)S(1)} %add_rsqrt_fusion.2, f32[256]{0:T(256)S(1)} %broadcast_multiply_fusion.2, bf16[2,256,1536]{2,1,0:T(8,128)(2,1)} %param.10), kind=kOutput, calls=%fused_computation.45 | convolution fusion | flops 1814888448 | bytes 9058304 | tf_op jit(solution)/shard_map/dot_general | solution.py:84
  293.3 23.1 %all-gather.7.cloned.1.call-done = bf16[1024,1536]{1,0:T(8,128)(2,1)} async-done(((bf16[256,1536]{1,0:T(8,128)(2,1)}), bf16[1024,1536]{1,0:T(8,128)(2,1)}) %all-gather.7.cloned.1.call-update) | async-done | bytes 3145744 | tf_op jit(solution)/shard_map/all_gather | solution.py:82
  316.4 3.9 copy.73
  323.4 3.9 copy.53
  327.3 4.0 copy.51
  331.3 29.1 %all-gather.9.cloned.1.call-done = bf16[1024,1536]{1,0:T(8,128)(2,1)} async-done(((bf16[256,1536]{1,0:T(8,128)(2,1)}), bf16[1024,1536]{1,0:T(8,128)(2,1)}) %all-gather.9.cloned.1.call-update) | async-done | bytes 3145744 | tf_op jit(solution)/shard_map/all_gather | solution.py:82
  360.4 3.9 copy.72
  367.4 3.9 copy.57
  371.4 4.1 copy.55
  375.4 6.9 %fusion.178 = f32[12,256]{1,0:T(8,128)S(1)} fusion(pred[1184]{0:T(1024)(128)(4,1)S(1)} %concatenate.35, bf16[256,12,64]{0,2,1:T(8,128)(2,1)} %bitcast.232, bf16[1184,12,64]{0,2,1:T(8,128)(2,1)} %bitcast.216), kind=kOutput, calls=%fused_computation.243 | convolution fusion | flops 480117920 | bytes 2225312 | tf_op jit(solution)/shard_map/sub | solution.py:38
  382.3 9.5 %fusion.93 = bf16[12,64,256]{2,1,0:T(8,128)(2,1)} fusion(bf16[1184,12,64]{0,2,1:T(8,128)(2,1)} %bitcast.218, f32[12,256]{1,0:T(8,128)S(1)} %fusion.178, pred[1184]{0:T(1024)(128)(4,1)S(1)} %concatenate.35, bf16[256,12,64]{0,2,1:T(8,128)(2,1)} %bitcast.233, bf16[1184,12,64]{0,2,1:T(8,128)(2,1)} %bitcast.217), kind=kOutput, calls=%fused_computation.131 | convolution fusion | flops 949522560 | bytes 4437152 | tf_op jit(solution)/shard_map/hqk,khd->qhd/dot_general | solution.py:40
  391.8 7.1 %fusion.177 = f32[12,256]{1,0:T(8,128)S(1)} fusion(pred[1184]{0:T(1024)(128)(4,1)S(1)} %concatenate.37, bf16[256,12,64]{0,2,1:T(8,128)(2,1)} %bitcast.234, bf16[1184,12,64]{0,2,1:T(8,128)(2,1)} %bitcast.223), kind=kOutput, calls=%fused_computation.242 | convolution fusion | flops 480117920 | bytes 2225312 | tf_op jit(solution)/shard_map/sub | solution.py:38
  398.9 9.4 %fusion.92 = bf16[12,64,256]{2,1,0:T(8,128)(2,1)} fusion(bf16[1184,12,64]{0,2,1:T(8,128)(2,1)} %bitcast.227, f32[12,256]{1,0:T(8,128)S(1)} %fusion.177, pred[1184]{0:T(1024)(128)(4,1)S(1)} %concatenate.37, bf16[256,12,64]{0,2,1:T(8,128)(2,1)} %bitcast.235, bf16[1184,12,64]{0,2,1:T(8,128)(2,1)} %bitcast.224), kind=kOutput, calls=%fused_computation.130 | convolution fusion | flops 949522560 | bytes 4437152 | tf_op jit(solution)/shard_map/hqk,khd->qhd/dot_general | solution.py:40
  414.3 4.0 collective-permute-done
  426.0 3.5 pad_maximum_fusion
  429.5 4.0 copy.63
  433.7 4.1 copy.61
  437.7 4.0 copy.60
  441.9 4.1 copy.58
  446.0 6.7 %fusion.180 = f32[12,256]{1,0:T(8,128)S(1)} fusion(pred[1184]{0:T(1024)(128)(4,1)S(1)} %copy-done.30, bf16[256,12,64]{0,2,1:T(8,128)(2,1)S(1)} %bitcast.238, bf16[1184,12,64]{0,2,1:T(8,128)(2,1)} %bitcast.221), kind=kOutput, calls=%fused_computation.245 | convolution fusion | flops 480117920 | bytes 2225312 | tf_op jit(solution)/shard_map/sub | solution.py:38
  452.7 8.7 %fusion.90 = bf16[12,64,256]{2,1,0:T(8,128)(2,1)S(1)} fusion(bf16[1184,12,64]{0,2,1:T(8,128)(2,1)} %bitcast.225, f32[12,256]{1,0:T(8,128)S(1)} %fusion.180, pred[1184]{0:T(1024)(128)(4,1)S(1)} %copy-done.30, bf16[256,12,64]{0,2,1:T(8,128)(2,1)} %bitcast.239, bf16[1184,12,64]{0,2,1:T(8,128)(2,1)} %bitcast.222), kind=kOutput, calls=%fused_computation.128 | convolution fusion | flops 949522560 | bytes 4437152 | tf_op jit(solution)/shard_map/hqk,khd->qhd/dot_general | solution.py:40
  461.4 7.0 %fusion.179 = f32[12,256]{1,0:T(8,128)S(1)} fusion(pred[1184]{0:T(1024)(128)(4,1)S(1)} %copy-done.28, bf16[256,12,64]{0,2,1:T(8,128)(2,1)S(1)} %bitcast.236, bf16[1184,12,64]{0,2,1:T(8,128)(2,1)} %bitcast.219), kind=kOutput, calls=%fused_computation.244 | convolution fusion | flops 480117920 | bytes 2225312 | tf_op jit(solution)/shard_map/sub | solution.py:38
  468.4 9.3 %fusion.91 = bf16[12,64,256]{2,1,0:T(8,128)(2,1)} fusion(bf16[1184,12,64]{0,2,1:T(8,128)(2,1)} %bitcast.226, f32[12,256]{1,0:T(8,128)S(1)} %fusion.179, pred[1184]{0:T(1024)(128)(4,1)S(1)} %copy-done.28, bf16[256,12,64]{0,2,1:T(8,128)(2,1)S(1)} %bitcast.237, bf16[1184,12,64]{0,2,1:T(8,128)(2,1)} %bitcast.220), kind=kOutput, calls=%fused_computation.129 | convolution fusion | flops 949522560 | bytes 4437152 | tf_op jit(solution)/shard_map/hqk,khd->qhd/dot_general | solution.py:40
  482.4 3.1 collective-permute-start.1
  485.8 2.7 maximum_select_fusion
  (136 shorter events, 51.1 us)
Async XLA Ops:
  7.2 149.3 %all-gather.11.cloned.1.call-start = ((), (), s32[]{:S(2)}) async-start(), calls=%async_computation.2 | async-start | bytes 14266368 | tf_op jit(solution)/shard_map/all_gather | solution.py:59
  8.8 263.1 %all-gather.13.cloned.1.call-start = ((), (), s32[]{:S(2)}) async-start(), calls=%async_computation.3 | async-start | bytes 4755456 | tf_op jit(solution)/shard_map/all_gather | solution.py:60
  10.3 306.1 %all-gather.7.cloned.1.call-start = ((), (), s32[]{:S(2)}) async-start(), calls=%async_computation | async-start | bytes 3932160 | tf_op jit(solution)/shard_map/all_gather | solution.py:82
  15.7 149.7 %copy-start.23 = (bf16[1,2,24,1536]{3,2,1,0:T(8,128)(2,1)S(1)}, bf16[1,2,24,1536]{3,2,1,0:T(8,128)(2,1)}, u32[]{:S(2)}) copy-start(bf16[1,2,24,1536]{3,2,1,0:T(8,128)(2,1)} %param.17) | copy-start | bytes 442372
  170.6 189.7 %all-gather.9.cloned.1.call-start = ((), (), s32[]{:S(2)}) async-start(), calls=%async_computation.1 | async-start | bytes 3932160 | tf_op jit(solution)/shard_map/all_gather | solution.py:82
  173.9 2.6 copy-start.31
  173.9 4.5 copy-start
  177.8 204.5 %copy-start.27 = (pred[1184]{0:T(1024)(128)(4,1)}, pred[1184]{0:T(1024)(128)(4,1)S(1)}, u32[]{:S(2)}) copy-start(pred[1184]{0:T(1024)(128)(4,1)S(1)} %concatenate.35) | copy-start | bytes 3556
  178.4 220.5 %copy-start.29 = (pred[1184]{0:T(1024)(128)(4,1)}, pred[1184]{0:T(1024)(128)(4,1)S(1)}, u32[]{:S(2)}) copy-start(pred[1184]{0:T(1024)(128)(4,1)S(1)} %concatenate.37) | copy-start | bytes 3556
  271.9 3.0 copy-start.1
  316.4 3.9 copy-start.6
  316.4 3.9 copy-start.22
  360.4 3.9 copy-start.7
  360.4 3.9 copy-start.20
  408.3 2.2 copy-start.2
  408.3 10.9 %slice-start = ((s8[7077888]{0:T(1024)(128)(4,1)}), s8[4194304]{0:T(1024)(128)(4,1)S(1)}, s32[]{:S(2)}) async-start(s8[7077888]{0:T(1024)(128)(4,1)} %bitcast.212), calls=%async_computation.4 | async-start | bytes 8388608
  410.5 8.7 %slice-start.1 = ((s8[7077888]{0:T(1024)(128)(4,1)}), s8[2883584]{0:T(1024)(128)(4,1)S(1)}, s32[]{:S(2)}) async-start(s8[7077888]{0:T(1024)(128)(4,1)} %bitcast.212), calls=%async_computation.5 | async-start | bytes 5767168
  413.0 5.3 %collective-permute-start = (bf16[2,256,1536]{2,1,0:T(8,128)(2,1)S(1)}, bf16[2,256,1536]{2,1,0:T(8,128)(2,1)S(1)}, u32[]{:S(2)}, u32[]{:S(2)}) collective-permute-start(bf16[2,256,1536]{2,1,0:T(8,128)(2,1)S(1)} %pad_maximum_fusion.4), channel_id=1, source_target_pairs={{0,128},{1,129},{2,130},{3,131},{4,132},{5,133},{6,134},{7,135},{8... | collective-permute-start | bytes 4718600 | tf_op jit(solution)/shard_map/ppermute | solution.py:14
  418.3 4.4 copy-start.4
  424.9 4.6 copy-start.18
  429.5 4.0 slice-start.2
  433.7 12.3 %copy-start.25 = (bf16[256,768]{0,1:T(8,128)(2,1)}, bf16[256,768]{0,1:T(8,128)(2,1)S(1)}, u32[]{:S(2)}) copy-start(bf16[256,768]{0,1:T(8,128)(2,1)S(1)} %copy.62) | copy-start | bytes 1179652
  437.7 4.0 slice-start.3
  441.9 4.1 copy-start.30
  452.7 8.7 %copy-start.28 = (pred[1184]{0:T(1024)(128)(4,1)S(1)}, pred[1184]{0:T(1024)(128)(4,1)}, u32[]{:S(2)}) copy-start(pred[1184]{0:T(1024)(128)(4,1)} %copy-done.27) | copy-start | bytes 3556
  481.5 4.1 copy-start.26
  481.5 4.2 copy-start.14
  481.5 4.2 copy-start.15
  481.5 4.3 copy-start.16
  482.4 6.0 %collective-permute-start.1 = (bf16[2,256,768]{2,1,0:T(8,128)(2,1)}, bf16[2,256,768]{2,1,0:T(8,128)(2,1)}, u32[]{:S(2)}, u32[]{:S(2)}) collective-permute-start(bf16[2,256,768]{2,1,0:T(8,128)(2,1)} %fusion.94), channel_id=1, source_target_pairs={{128,0},{129,1},{130,2},{131,3},{132,4},{133,5},{134,6},{135,7},{1... | collective-permute-start | bytes 2359304 | tf_op jit(solution)/shard_map/ppermute | solution.py:14
  485.7 2.7 copy-start.3
  485.7 2.7 copy-start.11
  (10 other events, 14.5 us)
Sparse Core Ops, SparseCore 0:
  12.3 144.0 all-gather.10
  160.8 111.1 all-gather.12
  273.7 42.6 all-gather.6
  318.1 42.2 all-gather.8
where the time goes:
time: 502 us; the launch traced here: 497 us
  waiting for transfers between devices  288 us (57%)
  matrix products  93.5 us (19%)
  local copies, waits for them, and re-layouts  76.1 us (15%)
  other arithmetic  19.8 us (4%)
  between operations  14.6 us (3%)
    all_gather x1, waiting for transfers between devices, body(): lax.all_gather(w_qkv[0], ('patch', 'req'), axis=0, tiled=True)  141 us
    all_gather x1, waiting for transfers between devices, body(): lax.all_gather(w_out[0], ('patch', 'req'), axis=0, tiled=True)  91.4 us
    all_gather x2, waiting for transfers between devices, process(): image_rows = lax.all_gather(patched, 'patch', axis=0, tiled=True)  52.2 us
    dot_general x4, matrix products, attend(): jnp.einsum('hqk,khd->qhd', soft_weights, value_heads, preferred_element_t...  36.9 us
    unnamed x74, local copies, waits for them, and re-layouts  27.8 us
    sub x4, matrix products, attend(): exp_scores = jnp.exp(scores - row_max)  27.6 us
    slice x4, local copies, waits for them, and re-layouts, process(): context[:, head_width:]  16.2 us
    slice x4, local copies, waits for them, and re-layouts, process(): context[:, :head_width]  15.8 us
  transfers between devices with their start and end apart: 6, of which 5 were waited for; matrix products, arithmetic and copies ran while one was open for 13% of the time, Pallas kernels for 0%

commit v1 on v0

--- a/solution.py
+++ b/solution.py
@@ -6,6 +6,13 @@
 HEADS = 12
 norm_eps = 1e-06
 score_scale = 0.125
+
+
+def deliver_area(xin, out_dim):
+    q_next = lax.axis_size("patch")
+    piece_next = jnp.stack(q_next * [xin])
+    taken_in = lax.all_to_all(piece_next, axis_name="patch", split_axis=0, concat_axis=0)
+    return jnp.concatenate(taken_in, axis=out_dim)
 
 
 def shifted(block, axis, distance):
@@ -79,7 +86,7 @@
             held_norm, full_qkv[:, head_width:], preferred_element_type=jnp.float32
         ).astype(jnp.bfloat16)
         patched = stale_block.at[redo_index].set(redone)
-        image_rows = lax.all_gather(patched, "patch", axis=0, tiled=True)
+        image_rows = deliver_area(patched, 0)
         normed = modulate(layer_input, mod_rows[0], mod_rows[1])
         projected = jnp.dot(normed, full_qkv, preferred_element_type=jnp.float32).astype(
             jnp.bfloat16

time: 502 us -> 456 us (0.908)
  waiting for transfers between devices: 288 us -> 226 us
  starting transfers between devices: 4.55 us -> 13.6 us
    all_gather x2 -> x0, waiting for transfers between devices: 52.2 us -> none  [process(): image_rows = lax.all_gather(patched, 'patch', axis=0, tiled=True)]
    all_gather x1, waiting for transfers between devices: 91.4 us -> 56.6 us  [body(): lax.all_gather(w_out[0], ('patch', 'req'), axis=0, tiled=True)]
    all_to_all x0 -> x2, waiting for transfers between devices: none -> 25.7 us  [deliver_area(): lax.all_to_all(piece_next, axis_name='patch', split_axis=0, concat_axis=0)]
    all_to_all x0 -> x2, starting transfers between devices: none -> 9.14 us  [deliver_area(): lax.all_to_all(piece_next, axis_name='patch', split_axis=0, concat_axis=0)]
    another operation x0 -> x2, local copies, waits for them, and re-layouts: none -> 5.52 us  [deliver_area(): piece_next = jnp.stack(q_next * [xin])]
  transfers between devices with their start and end apart: 6 -> 6, of which waited for: 5 -> 4; matrix products, arithmetic and copies ran while one was open for 13% -> 16% of each run, Pallas kernels for 0% -> 0%
where the time goes in v1:
time: 456 us; the launch traced here: 450 us
  waiting for transfers between devices  226 us (50%)
  matrix products  93.1 us (20%)
  local copies, waits for them, and re-layouts  79.4 us (17%)
  other arithmetic  23.2 us (5%)
  between operations  14.8 us (3%)
  starting transfers between devices  13.6 us (3%)
    all_gather x1, waiting for transfers between devices, body(): lax.all_gather(w_qkv[0], ('patch', 'req'), axis=0, tiled=True)  139 us
    all_gather x1, waiting for transfers between devices, body(): lax.all_gather(w_out[0], ('patch', 'req'), axis=0, tiled=True)  56.6 us
    dot_general x4, matrix products, attend(): jnp.einsum('hqk,khd->qhd', soft_weights, value_heads, preferred_element_t...  36.9 us
    sub x4, matrix products, attend(): exp_scores = jnp.exp(scores - row_max)  27.6 us
    unnamed x74, local copies, waits for them, and re-layouts  26.2 us
    all_to_all x2, waiting for transfers between devices, deliver_area(): lax.all_to_all(piece_next, axis_name='patch', split_axis=0, concat_axis=0)  25.7 us
    slice x4, local copies, waits for them, and re-layouts, process(): context[:, head_width:]  16.2 us
    slice x4, local copies, waits for them, and re-layouts, process(): context[:, :head_width]  15.8 us
  transfers between devices with their start and end apart: 6, of which 4 were waited for; matrix products, arithmetic and copies ran while one was open for 16% of the time, Pallas kernels for 0%

profile of v1, /device:TPU:1, one launch (start us, length us, event | category | flops | bytes accessed | tf_op | source)
XLA Modules:
  0.0 450.0 jit_solution(12473100011457481354)
XLA Ops:
  17.9 138.6 %all-gather.5.cloned.1.call-done = bf16[1,1536,2304]{2,0,1:T(2,128)(2,1)} async-done(((bf16[1,12,2304]{2,0,1:T(2,128)(2,1)}), bf16[1,1536,2304]{2,0,1:T(2,128)(2,1)}) %all-gather.5.cloned.1.call-update) | async-done | bytes 7077904 | tf_op jit(solution)/shard_map/all_gather | solution.py:66
  156.4 9.0 %copy.67 = bf16[1,1536,2304]{2,1,0:T(8,128)(2,1)} copy(bf16[1,1536,2304]{2,0,1:T(2,128)(2,1)} %all-gather.5.cloned.1.call-done) | data formatting | bytes 14155776
  165.5 3.1 fusion.52
  171.7 4.0 all-to-all-start
  180.5 3.1 fusion.55
  186.5 25.7 %all-to-all-done = bf16[4,256,1536]{2,1,0:T(8,128)(2,1)S(1)} async-done(((bf16[4,256,1536]{2,1,0:T(8,128)(2,1)}), bf16[4,256,1536]{2,1,0:T(8,128)(2,1)S(1)}, u32[]{:S(2)}, u32[]{:S(2)}) %all-to-all-start) | async-done | bytes 3145760 | tf_op jit(solution)/shard_map/all_to_all | solution.py:14
  212.1 3.6 stack.30
  215.8 5.2 %all-to-all-start.1 = ((bf16[4,256,1536]{2,1,0:T(8,128)(2,1)}), bf16[4,256,1536]{2,1,0:T(8,128)(2,1)}, u32[]{:S(2)}, u32[]{:S(2)}) async-start(bf16[4,256,1536]{2,1,0:T(8,128)(2,1)} %stack.30), calls=%async_computation.1 | async-start | bytes 6291456 | tf_op jit(solution)/shard_map/all_to_all | solution.py:14
  221.0 56.6 %all-gather.7.cloned.1.call-done = bf16[1,768,1536]{2,0,1:T(2,128)(2,1)} async-done(((bf16[1,6,1536]{2,0,1:T(2,128)(2,1)}), bf16[1,768,1536]{2,0,1:T(2,128)(2,1)}) %all-gather.7.cloned.1.call-update) | async-done | bytes 2359312 | tf_op jit(solution)/shard_map/all_gather | solution.py:67
  280.6 5.2 %convolution_convert_fusion.3 = bf16[256,2304]{1,0:T(8,128)(2,1)S(1)} fusion(bf16[1536,2304]{1,0:T(8,128)(2,1)} %bitcast.214, f32[1536]{0:T(1024)S(1)} %get-tuple-element.16, f32[1536]{0:T(1024)S(1)} %get-tuple-element.17, f32[256]{0:T(256)S(1)} %add_rsqrt_fusion.3, f32[256]{0:T(256)S(1)} %broadcast_multiply_fusion.3, bf16[2,256,1536]{2,1,0:T(8,128)(2,1)S(1)} %copy-done.3), kind=kOutput, calls=%fused_computation.46 | convolution fusion | flops 1814888448 | bytes 9062400 | tf_op jit(solution)/shard_map/dot_general | solution.py:91
  287.7 5.4 %convolution_convert_fusion.2 = bf16[256,2304]{1,0:T(8,128)(2,1)S(1)} fusion(bf16[1536,2304]{1,0:T(8,128)(2,1)} %bitcast.215, f32[1536]{0:T(1024)S(1)} %get-tuple-element.18, f32[1536]{0:T(1024)S(1)} %get-tuple-element.19, f32[256]{0:T(256)S(1)} %add_rsqrt_fusion.2, f32[256]{0:T(256)S(1)} %broadcast_multiply_fusion.2, bf16[2,256,1536]{2,1,0:T(8,128)(2,1)} %param.10), kind=kOutput, calls=%fused_computation.45 | convolution fusion | flops 1814888448 | bytes 9058304 | tf_op jit(solution)/shard_map/dot_general | solution.py:91
  295.1 4.0 copy.73
  302.2 3.9 copy.53
  306.1 3.9 copy.51
  310.1 3.8 copy.72
  315.2 3.9 pad_maximum_fusion.1
  319.2 3.9 copy.57
  323.1 4.1 copy.55
  327.2 6.9 %fusion.178 = f32[12,256]{1,0:T(8,128)S(1)} fusion(pred[1184]{0:T(1024)(128)(4,1)S(1)} %concatenate.35, bf16[256,12,64]{0,2,1:T(8,128)(2,1)} %bitcast.236, bf16[1184,12,64]{0,2,1:T(8,128)(2,1)} %bitcast.220), kind=kOutput, calls=%fused_computation.243 | convolution fusion | flops 480117920 | bytes 2225312 | tf_op jit(solution)/shard_map/sub | solution.py:45
  334.1 9.4 %fusion.93 = bf16[12,64,256]{2,1,0:T(8,128)(2,1)} fusion(bf16[1184,12,64]{0,2,1:T(8,128)(2,1)} %bitcast.222, f32[12,256]{1,0:T(8,128)S(1)} %fusion.178, pred[1184]{0:T(1024)(128)(4,1)S(1)} %concatenate.35, bf16[256,12,64]{0,2,1:T(8,128)(2,1)} %bitcast.237, bf16[1184,12,64]{0,2,1:T(8,128)(2,1)} %bitcast.221), kind=kOutput, calls=%fused_computation.131 | convolution fusion | flops 949522560 | bytes 4437152 | tf_op jit(solution)/shard_map/hqk,khd->qhd/dot_general | solution.py:47
  343.5 7.1 %fusion.177 = f32[12,256]{1,0:T(8,128)S(1)} fusion(pred[1184]{0:T(1024)(128)(4,1)S(1)} %concatenate.37, bf16[256,12,64]{0,2,1:T(8,128)(2,1)} %bitcast.238, bf16[1184,12,64]{0,2,1:T(8,128)(2,1)} %bitcast.227), kind=kOutput, calls=%fused_computation.242 | convolution fusion | flops 480117920 | bytes 2225312 | tf_op jit(solution)/shard_map/sub | solution.py:45
  350.6 9.5 %fusion.92 = bf16[12,64,256]{2,1,0:T(8,128)(2,1)} fusion(bf16[1184,12,64]{0,2,1:T(8,128)(2,1)} %bitcast.231, f32[12,256]{1,0:T(8,128)S(1)} %fusion.177, pred[1184]{0:T(1024)(128)(4,1)S(1)} %concatenate.37, bf16[256,12,64]{0,2,1:T(8,128)(2,1)} %bitcast.239, bf16[1184,12,64]{0,2,1:T(8,128)(2,1)} %bitcast.228), kind=kOutput, calls=%fused_computation.130 | convolution fusion | flops 949522560 | bytes 4437152 | tf_op jit(solution)/shard_map/hqk,khd->qhd/dot_general | solution.py:47
  366.1 5.0 %collective-permute-done = bf16[2,256,1536]{2,1,0:T(8,128)(2,1)S(1)} collective-permute-done((bf16[2,256,1536]{2,1,0:T(8,128)(2,1)S(1)}, bf16[2,256,1536]{2,1,0:T(8,128)(2,1)S(1)}, u32[]{:S(2)}, u32[]{:S(2)}) %collective-permute-start) | collective-permute-done | bytes 1572896 | tf_op jit(solution)/shard_map/ppermute | solution.py:21
  378.9 3.5 pad_maximum_fusion
  382.4 4.0 copy.63
  386.6 4.1 copy.61
  390.6 4.0 copy.60
  394.8 4.1 copy.58
  398.9 6.7 %fusion.180 = f32[12,256]{1,0:T(8,128)S(1)} fusion(pred[1184]{0:T(1024)(128)(4,1)S(1)} %copy-done.31, bf16[256,12,64]{0,2,1:T(8,128)(2,1)S(1)} %bitcast.242, bf16[1184,12,64]{0,2,1:T(8,128)(2,1)} %bitcast.225), kind=kOutput, calls=%fused_computation.245 | convolution fusion | flops 480117920 | bytes 2225312 | tf_op jit(solution)/shard_map/sub | solution.py:45
  405.6 8.7 %fusion.90 = bf16[12,64,256]{2,1,0:T(8,128)(2,1)S(1)} fusion(bf16[1184,12,64]{0,2,1:T(8,128)(2,1)} %bitcast.229, f32[12,256]{1,0:T(8,128)S(1)} %fusion.180, pred[1184]{0:T(1024)(128)(4,1)S(1)} %copy-done.31, bf16[256,12,64]{0,2,1:T(8,128)(2,1)} %bitcast.243, bf16[1184,12,64]{0,2,1:T(8,128)(2,1)} %bitcast.226), kind=kOutput, calls=%fused_computation.128 | convolution fusion | flops 949522560 | bytes 4437152 | tf_op jit(solution)/shard_map/hqk,khd->qhd/dot_general | solution.py:47
  414.3 7.0 %fusion.179 = f32[12,256]{1,0:T(8,128)S(1)} fusion(pred[1184]{0:T(1024)(128)(4,1)S(1)} %copy-done.29, bf16[256,12,64]{0,2,1:T(8,128)(2,1)S(1)} %bitcast.240, bf16[1184,12,64]{0,2,1:T(8,128)(2,1)} %bitcast.223), kind=kOutput, calls=%fused_computation.244 | convolution fusion | flops 480117920 | bytes 2225312 | tf_op jit(solution)/shard_map/sub | solution.py:45
  421.3 9.3 %fusion.91 = bf16[12,64,256]{2,1,0:T(8,128)(2,1)} fusion(bf16[1184,12,64]{0,2,1:T(8,128)(2,1)} %bitcast.230, f32[12,256]{1,0:T(8,128)S(1)} %fusion.179, pred[1184]{0:T(1024)(128)(4,1)S(1)} %copy-done.29, bf16[256,12,64]{0,2,1:T(8,128)(2,1)S(1)} %bitcast.241, bf16[1184,12,64]{0,2,1:T(8,128)(2,1)} %bitcast.224), kind=kOutput, calls=%fused_computation.129 | convolution fusion | flops 949522560 | bytes 4437152 | tf_op jit(solution)/shard_map/hqk,khd->qhd/dot_general | solution.py:47
  (136 shorter events, 59.0 us)
Async XLA Ops:
  7.2 149.3 %all-gather.5.cloned.1.call-start = ((), (), s32[]{:S(2)}) async-start(), calls=%async_computation.2 | async-start | bytes 14266368 | tf_op jit(solution)/shard_map/all_gather | solution.py:66
  8.8 268.7 %all-gather.7.cloned.1.call-start = ((), (), s32[]{:S(2)}) async-start(), calls=%async_computation.3 | async-start | bytes 4755456 | tf_op jit(solution)/shard_map/all_gather | solution.py:67
  17.9 147.6 %copy-start.24 = (bf16[1,2,24,1536]{3,2,1,0:T(8,128)(2,1)S(1)}, bf16[1,2,24,1536]{3,2,1,0:T(8,128)(2,1)}, u32[]{:S(2)}) copy-start(bf16[1,2,24,1536]{3,2,1,0:T(8,128)(2,1)} %param.17) | copy-start | bytes 442372
  171.7 40.4 %all-to-all-start = ((bf16[4,256,1536]{2,1,0:T(8,128)(2,1)}), bf16[4,256,1536]{2,1,0:T(8,128)(2,1)S(1)}, u32[]{:S(2)}, u32[]{:S(2)}) async-start(bf16[4,256,1536]{2,1,0:T(8,128)(2,1)} %stack.28), calls=%async_computation | async-start | bytes 6291456 | tf_op jit(solution)/shard_map/all_to_all | solution.py:14
  176.4 157.7 %copy-start.28 = (pred[1184]{0:T(1024)(128)(4,1)}, pred[1184]{0:T(1024)(128)(4,1)S(1)}, u32[]{:S(2)}) copy-start(pred[1184]{0:T(1024)(128)(4,1)S(1)} %concatenate.35) | copy-start | bytes 3556
  177.0 173.6 %copy-start.30 = (pred[1184]{0:T(1024)(128)(4,1)}, pred[1184]{0:T(1024)(128)(4,1)S(1)}, u32[]{:S(2)}) copy-start(pred[1184]{0:T(1024)(128)(4,1)S(1)} %concatenate.37) | copy-start | bytes 3556
  177.0 2.4 copy-start.23
  212.1 3.6 copy-start
  215.8 94.3 %all-to-all-start.1 = ((bf16[4,256,1536]{2,1,0:T(8,128)(2,1)}), bf16[4,256,1536]{2,1,0:T(8,128)(2,1)}, u32[]{:S(2)}, u32[]{:S(2)}) async-start(bf16[4,256,1536]{2,1,0:T(8,128)(2,1)} %stack.30), calls=%async_computation.1 | async-start | bytes 6291456 | tf_op jit(solution)/shard_map/all_to_all | solution.py:14
  277.5 3.0 copy-start.3
  295.1 4.0 copy-start.1
  295.1 4.0 copy-start.22
  310.1 3.9 copy-start.20
  360.1 2.2 copy-start.4
  360.1 11.9 %slice-start = ((s8[7077888]{0:T(1024)(128)(4,1)}), s8[4194304]{0:T(1024)(128)(4,1)S(1)}, s32[]{:S(2)}) async-start(s8[7077888]{0:T(1024)(128)(4,1)} %bitcast.216), calls=%async_computation.4 | async-start | bytes 8388608
  362.3 9.7 %slice-start.1 = ((s8[7077888]{0:T(1024)(128)(4,1)}), s8[2883584]{0:T(1024)(128)(4,1)S(1)}, s32[]{:S(2)}) async-start(s8[7077888]{0:T(1024)(128)(4,1)} %bitcast.216), calls=%async_computation.5 | async-start | bytes 5767168
  364.8 6.3 %collective-permute-start = (bf16[2,256,1536]{2,1,0:T(8,128)(2,1)S(1)}, bf16[2,256,1536]{2,1,0:T(8,128)(2,1)S(1)}, u32[]{:S(2)}, u32[]{:S(2)}) collective-permute-start(bf16[2,256,1536]{2,1,0:T(8,128)(2,1)S(1)} %pad_maximum_fusion.4), channel_id=1, source_target_pairs={{0,128},{1,129},{2,130},{3,131},{4,132},{5,133},{6,134},{7,135},{8... | collective-permute-start | bytes 4718600 | tf_op jit(solution)/shard_map/ppermute | solution.py:21
  371.2 4.4 copy-start.6
  372.1 2.2 copy-start.9
  377.8 4.6 %copy-start.18 = (bf16[256,2304]{1,0:T(8,128)(2,1)}, bf16[256,2304]{1,0:T(8,128)(2,1)S(1)}, u32[]{:S(2)}) copy-start(bf16[256,2304]{1,0:T(8,128)(2,1)S(1)} %convolution_convert_fusion.1) | copy-start | bytes 3538948
  382.4 4.0 slice-start.2
  386.6 12.3 %copy-start.26 = (bf16[256,768]{0,1:T(8,128)(2,1)}, bf16[256,768]{0,1:T(8,128)(2,1)S(1)}, u32[]{:S(2)}) copy-start(bf16[256,768]{0,1:T(8,128)(2,1)S(1)} %copy.62) | copy-start | bytes 1179652
  390.6 4.0 slice-start.3
  394.8 4.1 copy-start.31
  405.6 8.7 %copy-start.29 = (pred[1184]{0:T(1024)(128)(4,1)S(1)}, pred[1184]{0:T(1024)(128)(4,1)}, u32[]{:S(2)}) copy-start(pred[1184]{0:T(1024)(128)(4,1)} %copy-done.28) | copy-start | bytes 3556
  434.4 4.0 copy-start.27
  434.4 4.2 copy-start.14
  434.4 4.2 copy-start.15
  434.4 4.2 copy-start.16
  435.3 6.0 %collective-permute-start.1 = (bf16[2,256,768]{2,1,0:T(8,128)(2,1)}, bf16[2,256,768]{2,1,0:T(8,128)(2,1)}, u32[]{:S(2)}, u32[]{:S(2)}) collective-permute-start(bf16[2,256,768]{2,1,0:T(8,128)(2,1)} %fusion.94), channel_id=1, source_target_pairs={{128,0},{129,1},{130,2},{131,3},{132,4},{133,5},{134,6},{135,7},{1... | collective-permute-start | bytes 2359304 | tf_op jit(solution)/shard_map/ppermute | solution.py:21
  438.6 2.7 copy-start.5
  438.6 2.7 copy-start.11
  (10 other events, 14.9 us)
Sparse Core Ops, SparseCore 0:
  12.3 144.0 all-gather.4
  160.2 117.2 all-gather.6
